TPU v7x, 128 devices: a whole 4x4x4 slice. The times are simulated.
128 devices in a mesh: freq: 8 (over z_hi, x), blk: 16 (over y, z_lo, core).
Axes of the slice: x: 4, y: 4, z: 4 (z_hi: 2, z_lo: 2; z = z_hi * 2 + z_lo), core: 2. Of those that a mesh axis runs over, the one named last changes fastest.
Arguments:
- traces: bfloat16 [2048, 2048, 256], P('blk', 'freq'), may hold values from -6 to 6
- signature: float32 [8, 2], P('freq'), may hold values from 0.5 to 1.5
Outputs:
- multiples: float32 [8, 2, 2048, 2048], P('freq', None, 'blk')
All inputs are finite; a program needn't handle non-finite values.
Results may differ from a plain program's by a relative error of at most 0.0035.
Values sent between devices are 32-bit elements; how exact they have to be, the bound alone decides.
No kernel may reach another device: no remote copies, remote signals or barrier semaphores. Data moves between devices by JAX's collectives and lax.ppermute only.
A program may use at most 256 MiB of HBM per device.

v0:
```python
import math
import jax
import jax.numpy as jnp
from jax import lax
from jax.sharding import PartitionSpec as P

BIN0 = 4
BINSTEP = 3


def make_table(freqs, samples):
    bins = BIN0 + BINSTEP * jnp.arange(freqs, dtype=jnp.int32)
    steps = jnp.arange(samples, dtype=jnp.int32)
    phase = steps[:, None] * bins[None, :] % samples
    angle = phase.astype(jnp.float32) * (2.0 * math.pi / samples)
    scale = 1.0 / math.sqrt(samples)
    table = jnp.concatenate([jnp.cos(angle) * scale, -jnp.sin(angle) * scale], axis=1)
    return table.astype(jnp.bfloat16)


def complex_dot(a_re, a_im, b_re, b_im):
    hp = lax.Precision.HIGHEST
    real_part = jnp.dot(a_re, b_re, precision=hp) - jnp.dot(a_im, b_im, precision=hp)
    imag_part = jnp.dot(a_re, b_im, precision=hp) + jnp.dot(a_im, b_re, precision=hp)
    return (real_part, imag_part)


def on_device(traces, signature):
    src_rows, rec_cols, samples = traces.shape
    freqs = lax.axis_size("freq")
    table = make_table(freqs, samples)
    projected = jnp.einsum("srt,tc->csr", traces, table, preferred_element_type=jnp.float32)
    projected = projected.reshape(2, freqs, src_rows, rec_cols)
    spectra = lax.all_to_all(projected, "freq", split_axis=1, concat_axis=3, tiled=True)
    own = spectra[:, 0]
    width = own.shape[2]
    own_re = own[0]
    own_im = own[1]
    full = lax.all_gather(own, "blk", axis=1, tiled=True)
    prod_re, prod_im = complex_dot(own_re, own_im, full[0], full[1])
    scale = 1.0 / math.sqrt(width)
    w_re = signature[0, 0]
    w_im = signature[0, 1]
    out_re = -(w_re * prod_re - w_im * prod_im) * scale
    out_im = -(w_re * prod_im + w_im * prod_re) * scale
    return jnp.stack([out_re, out_im], axis=0)[None]


def solution(mesh):
    return jax.shard_map(
        on_device,
        mesh=mesh,
        in_specs=(P("blk", "freq", None), P("freq", None)),
        out_specs=P("freq", None, "blk", None),
        check_vma=False,
    )
```

profile of v0, /device:TPU:1, one launch (start us, length us, event | category | flops | bytes accessed | tf_op | source)
XLA Modules:
  0.0 346.1 jit_solution(8752176337144553729)
XLA Ops:
  6.5 0.0 all-gather.2.cloned.1.call-start
  6.5 0.1 multiply_convert_fusion.1
  6.7 0.0 copy-start.1
  6.7 10.2 %convolution_bitcast_fusion = f32[2,8,128,256]{3,1,0,2:T(8,128)S(1)} fusion(bf16[128,256,256]{2,1,0:T(8,128)(2,1)} %param.2, bf16[256,8]{0,1:T(8,128)(2,1)S(1)} %get-tuple-element.14, bf16[256,8]{0,1:T(8,128)(2,1)S(1)} %get-tuple-element.13), kind=kOutput, calls=%fused_computation.15 | convolution fusion | flops 268451840 | bytes 18882560 | tf_op jit(solution)/shard_map/srt,tc->csr/dot_general | solution.py:32
  16.9 1.1 copy.4
  18.0 36.3 %all_to_all.15 = f32[2,8,128,256]{3,0,2,1:T(2,128)} all-to-all(f32[2,8,128,256]{3,0,2,1:T(2,128)S(1)} %copy.4), channel_id=1, replica_groups=mesh['freq'=8,'blk'=16] {'freq'}, dimensions={1} | all-to-all | bytes 4194304 | tf_op jit(solution)/shard_map/all_to_all | solution.py:34
  54.3 2.7 copy.5
  57.0 2.3 copy.6
  59.4 0.0 all-gather.2.cloned.1.call-update
  59.4 0.0 copy-done.1
  59.4 0.7 fusion.29
  60.1 1.1 fusion.28
  61.2 168.2 %all-gather.2.cloned.1.call-done = f32[2,2048,2048]{2,0,1:T(2,128)} async-done(((f32[2,128,2048]{2,0,1:T(2,128)}), f32[2,2048,2048]{2,0,1:T(2,128)}) %all-gather.2.cloned.1.call-update) | async-done | bytes 33554448 | tf_op jit(solution)/shard_map/all_gather | solution.py:39
  229.4 40.0 %fusion.27 = (f32[1,2048,2048]{2,0,1:T(1,128)}, f32[1,2048,2048]{2,0,1:T(1,128)}) fusion(f32[2,2048,2048]{2,0,1:T(2,128)} %all-gather.2.cloned.1.call-done), kind=kLoop, calls=%fused_computation.34 | loop fusion | bytes 67108864 | tf_op jit(solution)/shard_map/slice | solution.py:40
  269.4 0.0 slice-start
  269.4 0.0 slice-start.1
  269.4 18.8 %fusion.2 = f32[128,2048]{1,0:T(8,128)S(1)} fusion(f32[128,2048]{0,1:T(8,128)S(1)} %bitcast.45, f32[1,2048,2048]{2,0,1:T(1,128)} %get-tuple-element.6), kind=kOutput, calls=%fused_computation.2 | convolution fusion | flops 6442450944 | bytes 18874368 | tf_op jit(solution)/shard_map/dot_general | solution.py:23
  288.2 0.0 slice-start.2
  288.2 0.0 copy-done
  288.2 0.0 slice-start.3
  288.2 19.2 %fusion = f32[128,2048]{1,0:T(8,128)S(1)} fusion(f32[128,2048]{0,1:T(8,128)S(1)} %bitcast.47, f32[1,2048,2048]{2,0,1:T(1,128)} %get-tuple-element.6), kind=kOutput, calls=%fused_computation | convolution fusion | flops 6442450944 | bytes 18874368 | tf_op jit(solution)/shard_map/dot_general | solution.py:24
  307.5 14.1 %fusion.12 = f32[128,2048]{1,0:T(8,128)S(1)} fusion(f32[128,2048]{1,0:T(8,128)S(1)} %fusion.2, f32[128,2048]{0,1:T(8,128)S(1)} %bitcast.48, f32[1,2048,2048]{2,0,1:T(1,128)S(1)} %bitcast.42), kind=kOutput, calls=%fused_computation.12 | convolution fusion | flops 6442713088 | bytes 19922944 | tf_op jit(solution)/shard_map/dot_general | solution.py:23
  321.6 15.7 %multiply_bitcast_fusion.1 = (f32[1,128,2048]{2,1,0:T(8,128)S(1)}, f32[1,128,2048]{2,1,0:T(8,128)S(1)}) fusion(f32[128,2048]{1,0:T(8,128)S(1)} %fusion.12, f32[]{:T(128)} %bitcast.9, f32[]{:T(128)} %bitcast, f32[128,2048]{1,0:T(8,128)S(1)} %fusion, f32[128,2048]{0,1:T(8,128)S(1)} %bitcast.46, f32[1,2048,2048]{2,0,1:T(1,128)S(1)} %bitcast.42), kind=kOutput, calls=%fused_computation.17 | convolution fusion | flops 6445334528 | bytes 22020104 | tf_op jit(solution)/shard_map/dot_general | solution.py:24
  337.3 1.5 maximum_bitcast_fusion
  (7 shorter events, 0.0 us)
Async XLA Ops:
  6.5 222.8 %all-gather.2.cloned.1.call-start = ((), (), s32[]{:S(2)}) async-start(), calls=%async_computation.1 | async-start | bytes 35651584 | tf_op jit(solution)/shard_map/all_gather | solution.py:39
  6.7 52.7 %copy-start.1 = (f32[1,2]{1,0:T(1,128)S(1)}, f32[1,2]{1,0:T(1,128)}, u32[]{:S(2)}) copy-start(f32[1,2]{1,0:T(1,128)} %param.3) | copy-start | bytes 28
  269.4 18.9 %copy-start = (f32[1,1,128,8,256]{2,4,3,1,0:T(8,128)S(1)}, f32[1,1,128,8,256]{2,4,3,1,0:T(8,128)}, u32[]{:S(2)}) copy-start(f32[1,1,128,8,256]{2,4,3,1,0:T(8,128)} %get-tuple-element.9) | copy-start | bytes 3145732
  269.4 38.1 %slice-start = ((s8[16777216]{0:T(1024)(128)(4,1)}), s8[4194304]{0:T(1024)(128)(4,1)S(1)}, s32[]{:S(2)}) async-start(s8[16777216]{0:T(1024)(128)(4,1)} %bitcast.41), calls=%async_computation.2 | async-start | bytes 8388608
  269.4 38.1 %slice-start.1 = ((s8[16777216]{0:T(1024)(128)(4,1)}), s8[4194304]{0:T(1024)(128)(4,1)S(1)}, s32[]{:S(2)}) async-start(s8[16777216]{0:T(1024)(128)(4,1)} %bitcast.41), calls=%async_computation.3 | async-start | bytes 8388608
  288.2 19.3 %slice-start.2 = ((s8[16777216]{0:T(1024)(128)(4,1)}), s8[4194304]{0:T(1024)(128)(4,1)S(1)}, s32[]{:S(2)}) async-start(s8[16777216]{0:T(1024)(128)(4,1)} %bitcast.41), calls=%async_computation.4 | async-start | bytes 8388608
  288.2 19.3 %slice-start.3 = ((s8[16777216]{0:T(1024)(128)(4,1)}), s8[4194304]{0:T(1024)(128)(4,1)S(1)}, s32[]{:S(2)}) async-start(s8[16777216]{0:T(1024)(128)(4,1)} %bitcast.41), calls=%async_computation.5 | async-start | bytes 8388608
Sparse Core Ops, SparseCore 0:
  59.5 169.8 all-gather.1
where the time goes:
time: 349 us; the launch traced here: 346 us
  waiting for transfers between devices  168 us (48%)
  matrix products  78 us (22%)
  local copies, waits for them, and re-layouts  48 us (14%)
  blocking collectives  36.3 us (10%)
  between operations  14 us (4%)
    all_gather x1, waiting for transfers between devices, on_device(): full = lax.all_gather(own, 'blk', axis=1, tiled=True)  168 us
    slice x1, local copies, waits for them, and re-layouts, on_device(): prod_re, prod_im = complex_dot(own_re, own_im, full[0], full[1])  40 us
    all_to_all x1, blocking collectives, on_device(): lax.all_to_all(projected, 'freq', split_axis=1, concat_axis=3, tiled=True)  36.3 us
    dot_general x1, matrix products, complex_dot(): jnp.dot(a_re, b_im, precision=hp) + jnp.dot(a_im, b_re, precision=hp)  19.2 us
    dot_general x1, matrix products, complex_dot(): jnp.dot(a_im, b_im, precision=hp)  18.8 us
    dot_general x1, matrix products, complex_dot(): jnp.dot(a_im, b_re, precision=hp)  15.7 us
    dot_general x1, matrix products, complex_dot(): jnp.dot(a_re, b_re, precision=hp) - jnp.dot(a_im, b_im, precision=hp)  14.1 us
    dot_general x1, matrix products, on_device(): jnp.einsum('srt,tc->csr', traces, table, preferred_element_type=jnp.float32)  10.2 us
  transfers between devices with their start and end apart: 1, of which 1 were waited for; matrix products, arithmetic and copies ran while one was open for 1% of the time, Pallas kernels for 0%

commit v1 on v0

--- a/solution.py
+++ b/solution.py
@@ -36,7 +36,15 @@
     width = own.shape[2]
     own_re = own[0]
     own_im = own[1]
-    full = lax.all_gather(own, "blk", axis=1, tiled=True)
+    full = jnp.concatenate(
+        lax.all_to_all(
+            jnp.stack([own for _ in range(lax.axis_size("blk"))], 0),
+            axis_name="blk",
+            split_axis=0,
+            concat_axis=0,
+        ),
+        1,
+    )
     prod_re, prod_im = complex_dot(own_re, own_im, full[0], full[1])
     scale = 1.0 / math.sqrt(width)
     w_re = signature[0, 0]

time: 349 us -> 688 us (1.97)
  waiting for transfers between devices: 168 us -> 546 us
  matrix products: 78 us -> 56 us
  between operations: 14 us -> 0.06 us
  local copies, waits for them, and re-layouts: 48 us -> 37.4 us
  starting transfers between devices: 0.01 us -> 7.56 us
    all_to_all x0 -> x1, waiting for transfers between devices: none -> 546 us  [on_device(): lax.all_to_all(jnp.stack([own for _ in range(lax.axis_size('blk'))], 0),...]
    all_gather x1 -> x0, waiting for transfers between devices: 168 us -> none  [on_device(): full = lax.all_gather(own, 'blk', axis=1, tiled=True)]
    slice x1, local copies, waits for them, and re-layouts: 40 us -> 17.8 us  [on_device(): prod_re, prod_im = complex_dot(own_re, own_im, full[0], full[1])]
    another operation x0 -> x2, local copies, waits for them, and re-layouts: none -> 14 us  [on_device(): jnp.stack([own for _ in range(lax.axis_size('blk'))], 0)]
    dot_general x1, matrix products: 19.2 us -> 9.06 us  [complex_dot(): jnp.dot(a_re, b_im, precision=hp) + jnp.dot(a_im, b_re, precision=hp)]
    dot_general x1, matrix products: 18.8 us -> 10.4 us  [complex_dot(): jnp.dot(a_im, b_im, precision=hp)]
    all_to_all x0 -> x1, starting transfers between devices: none -> 7.56 us  [on_device(): lax.all_to_all(jnp.stack([own for _ in range(lax.axis_size('blk'))], 0),...]
  transfers between devices with their start and end apart: 1 -> 1, of which waited for: 1 -> 1; matrix products, arithmetic and copies ran while one was open for 1% -> 0% of each run, Pallas kernels for 0% -> 0%
where the time goes in v1:
time: 688 us; the launch traced here: 685 us
  waiting for transfers between devices  546 us (79%)
  matrix products  56 us (8%)
  local copies, waits for them, and re-layouts  37.4 us (5%)
  blocking collectives  35.7 us (5%)
  starting transfers between devices  7.56 us (1%)
    all_to_all x1, waiting for transfers between devices, on_device(): lax.all_to_all(jnp.stack([own for _ in range(lax.axis_size('blk'))], 0),...  546 us
    all_to_all x1, blocking collectives, on_device(): lax.all_to_all(projected, 'freq', split_axis=1, concat_axis=3, tiled=True)  35.7 us
    slice x1, local copies, waits for them, and re-layouts, on_device(): prod_re, prod_im = complex_dot(own_re, own_im, full[0], full[1])  17.8 us
    another operation x2, local copies, waits for them, and re-layouts, on_device(): jnp.stack([own for _ in range(lax.axis_size('blk'))], 0)  14 us
  transfers between devices with their start and end apart: 1, of which 1 were waited for; matrix products, arithmetic and copies ran while one was open for 0% of the time, Pallas kernels for 0%

profile of v1, /device:TPU:1, one launch (start us, length us, event | category | flops | bytes accessed | tf_op | source)
XLA Modules:
  0.0 684.7 jit_solution(11935200161192306992)
XLA Ops:
  0.0 0.1 multiply_convert_fusion.1
  0.1 10.2 %convolution_bitcast_fusion = f32[2,8,128,256]{3,1,0,2:T(8,128)S(1)} fusion(bf16[128,256,256]{2,1,0:T(8,128)(2,1)} %param.2, bf16[256,8]{0,1:T(8,128)(2,1)S(1)} %get-tuple-element.14, bf16[256,8]{0,1:T(8,128)(2,1)S(1)} %get-tuple-element.13), kind=kOutput, calls=%fused_computation.3 | convolution fusion | flops 268451840 | bytes 18882560 | tf_op jit(solution)/shard_map/srt,tc->csr/dot_general | solution.py:32
  10.4 1.1 copy.5
  11.5 35.7 %all_to_all.20 = f32[2,8,128,256]{3,0,2,1:T(2,128)} all-to-all(f32[2,8,128,256]{3,0,2,1:T(2,128)S(1)} %copy.5), channel_id=1, replica_groups=mesh['freq'=8,'blk'=16] {'freq'}, dimensions={1} | all-to-all | bytes 4194304 | tf_op jit(solution)/shard_map/all_to_all | solution.py:34
  47.2 2.7 copy.6
  49.9 1.8 copy.7
  51.7 12.2 %stack.12 = f32[16,2,128,2048]{3,2,1,0:T(8,128)} broadcast(f32[2,128,2048]{2,1,0:T(8,128)} %copy.7), dimensions={1,2,3} | broadcast | bytes 35651584 | tf_op jit(solution)/shard_map/stack | solution.py:41
  63.9 0.0 copy-start.1
  63.9 7.6 %all-to-all-start.1 = ((f32[16,2,128,2048]{3,2,1,0:T(8,128)}), f32[16,2,128,2048]{3,2,1,0:T(8,128)}, u32[]{:S(2)}, u32[]{:S(2)}) async-start(f32[16,2,128,2048]{3,2,1,0:T(8,128)} %stack.12), calls=%async_computation.1 | async-start | bytes 67108864 | tf_op jit(solution)/shard_map/all_to_all | solution.py:40
  71.5 0.0 copy-done.1
  71.5 0.6 fusion.11
  72.1 1.1 fusion.10
  73.2 546.4 %all-to-all-done.1 = f32[16,2,128,2048]{3,2,1,0:T(8,128)} async-done(((f32[16,2,128,2048]{3,2,1,0:T(8,128)}), f32[16,2,128,2048]{3,2,1,0:T(8,128)}, u32[]{:S(2)}, u32[]{:S(2)}) %all-to-all-start.1) | async-done | bytes 33554464 | tf_op jit(solution)/shard_map/all_to_all | solution.py:40
  619.6 0.0 copy-start
  619.6 17.8 %fusion.9 = (f32[1,16,128,2048]{3,2,0,1:T(8,128)S(1)}, f32[1,16,128,2048]{3,2,0,1:T(8,128)}) fusion(f32[2,16,128,2048]{3,2,0,1:T(8,128)} %bitcast.8), kind=kLoop, calls=%fused_computation.22 | loop fusion | bytes 67108864 | tf_op jit(solution)/shard_map/slice | solution.py:48
  637.4 0.0 copy-done
  637.4 9.1 %fusion.13 = f32[128,2048]{1,0:T(8,128)S(1)} fusion(f32[128,2048]{0,1:T(8,128)S(1)} %bitcast.40, f32[2048,2048]{1,0:T(8,128)S(1)} %bitcast.32), kind=kOutput, calls=%fused_computation.26 | convolution fusion | flops 6442450944 | bytes 18874368 | tf_op jit(solution)/shard_map/dot_general | solution.py:24
  646.5 13.3 %fusion.12 = f32[128,2048]{1,0:T(8,128)S(1)} fusion(f32[128,2048]{0,1:T(8,128)S(1)} %bitcast.41, f32[2048,2048]{1,0:T(8,128)} %bitcast.34), kind=kOutput, calls=%fused_computation.25 | convolution fusion | flops 6442450944 | bytes 18874368 | tf_op jit(solution)/shard_map/dot_general | solution.py:23
  659.8 13.0 %convolution_add_fusion = f32[128,2048]{1,0:T(8,128)S(1)} fusion(f32[128,2048]{1,0:T(8,128)S(1)} %fusion.13, f32[128,2048]{0,1:T(8,128)S(1)} %bitcast.38, f32[2048,2048]{1,0:T(8,128)} %bitcast.35), kind=kOutput, calls=%fused_computation | convolution fusion | flops 6442713088 | bytes 19922944 | tf_op jit(solution)/shard_map/dot_general | solution.py:24
  672.8 10.4 %multiply_bitcast_fusion.1 = (f32[1,128,2048]{2,1,0:T(8,128)S(1)}, f32[1,128,2048]{2,1,0:T(8,128)S(1)}) fusion(f32[128,2048]{1,0:T(8,128)S(1)} %convolution_add_fusion, f32[]{:T(128)} %bitcast.12, f32[]{:T(128)} %bitcast, f32[128,2048]{1,0:T(8,128)S(1)} %fusion.12, f32[128,2048]{0,1:T(8,128)S(1)} %bitcast.39, f32[2048,2048]{1,0:T(8,128)S(1)} %bitcast.33), kind=kOutput, calls=%fused_computation.5 | convolution fusion | flops 6445334528 | bytes 22020104 | tf_op jit(solution)/shard_map/dot_general | solution.py:23
  683.2 1.5 maximum_bitcast_fusion
  (1 shorter events, 0.0 us)
Async XLA Ops:
  63.9 7.6 %copy-start.1 = (f32[1,2]{1,0:T(1,128)S(1)}, f32[1,2]{1,0:T(1,128)}, u32[]{:S(2)}) copy-start(f32[1,2]{1,0:T(1,128)} %param.3) | copy-start | bytes 28
  63.9 555.7 %all-to-all-start.1 = ((f32[16,2,128,2048]{3,2,1,0:T(8,128)}), f32[16,2,128,2048]{3,2,1,0:T(8,128)}, u32[]{:S(2)}, u32[]{:S(2)}) async-start(f32[16,2,128,2048]{3,2,1,0:T(8,128)} %stack.12), calls=%async_computation.1 | async-start | bytes 67108864 | tf_op jit(solution)/shard_map/all_to_all | solution.py:40
  619.6 17.8 %copy-start = (f32[1,1,128,8,256]{2,4,3,1,0:T(8,128)S(1)}, f32[1,1,128,8,256]{2,4,3,1,0:T(8,128)}, u32[]{:S(2)}) copy-start(f32[1,1,128,8,256]{2,4,3,1,0:T(8,128)} %get-tuple-element.10) | copy-start | bytes 3145732
